TPU v7x, 512 devices: a whole 4x8x8 slice. The times are simulated.
512 devices in a mesh: sk: 32 (over x, y), lang: 16 (over z, core).
Axes of the slice: x: 4, y: 8, z: 8, core: 2. Of those that a mesh axis runs over, the one named last changes fastest.
Arguments:
- embeddings: bfloat16 [524288, 1024], P(('sk', 'lang')), may hold values from -40 to 40
- omega: bfloat16 [524288, 256], P(('sk', 'lang')), may hold values from -0.0078125 to 0.0078125
- lang_ids: int32 [524288, 1], P(('sk', 'lang')), may hold values from 0 to 11; in each aligned block of 1024 rows (0 to 1023, 1024 to 2047, ...) at most 128 rows name the same one
Outputs:
- grouped: bfloat16 [1048576, 256], P(('sk', 'lang'))
Inputs may be any that keep to these rules, and one draw needn't show every extreme that they name: `lang_ids`: among the 1024 sentences of one device no language appears more than 128 times, and some language appears exactly 128 times.
All inputs are finite; a program needn't handle non-finite values.
Results may differ from a plain program's by a relative error of at most 0.0075.
Values may be sent and summed in bfloat16 or wider, within the bound.
No kernel may reach another device: no remote copies, remote signals or barrier semaphores. Data moves between devices by JAX's collectives and lax.ppermute only.
A program may use at most 64 MiB of HBM per device.

v0:
```python
import jax
import jax.numpy as jnp
from jax import lax
from jax.sharding import PartitionSpec as P

SKETCH = 256
LANGS = 12
CAP = 128


def orthonormal(term):
    sketch = lax.psum(term, ("sk", "lang"))
    gram_matrix = jnp.dot(
        sketch, sketch.T, precision=lax.Precision.HIGHEST, preferred_element_type=jnp.float32
    )
    lower_factor = jnp.linalg.cholesky(gram_matrix)
    return jax.scipy.linalg.solve_triangular(lower_factor, sketch, lower=True).astype(jnp.bfloat16)


def on_device(embeddings, omega, lang_ids):
    first_term = lax.dot_general(
        omega, embeddings, (((0,), (0,)), ((), ())), preferred_element_type=jnp.float32
    )
    first_basis = orthonormal(first_term)
    scores = lax.dot_general(
        embeddings, first_basis, (((1,), (1,)), ((), ())), preferred_element_type=jnp.float32
    ).astype(jnp.bfloat16)
    second_term = lax.dot_general(
        scores, embeddings, (((0,), (0,)), ((), ())), preferred_element_type=jnp.float32
    )
    second_basis = orthonormal(second_term)
    coords = lax.dot_general(
        embeddings, second_basis, (((1,), (1,)), ((), ())), preferred_element_type=jnp.float32
    ).astype(jnp.bfloat16)
    lang_count = lax.axis_size("lang")
    per_owner = (LANGS + lang_count - 1) // lang_count
    languages = lang_ids[:, 0]
    member = (languages[:, None] == jnp.arange(LANGS, dtype=jnp.int32)[None, :]).astype(jnp.int32)
    position = jnp.sum(jnp.cumsum(member, axis=0) * member, axis=1) - 1
    target = languages % lang_count * (per_owner * CAP) + languages // lang_count * CAP + position
    outgoing = (
        jnp.zeros((lang_count * per_owner * CAP, SKETCH), jnp.bfloat16).at[target].set(coords)
    )
    return lax.all_to_all(outgoing, "lang", split_axis=0, concat_axis=0, tiled=True)


def solution(mesh):
    in_specs = (P(("sk", "lang"), None), P(("sk", "lang"), None), P(("sk", "lang"), None))
    out_specs = P(("sk", "lang"), None)
    return jax.shard_map(
        on_device, mesh=mesh, in_specs=in_specs, out_specs=out_specs, check_vma=False
    )
```

profile of v0, /device:TPU:1, one launch (start us, length us, event | category | flops | bytes accessed | tf_op | source)
XLA Modules:
  0.0 760.9 jit_solution(11105118633514721056)
XLA Ops:
  6.5 1.6 copy-done
  8.1 2.7 fusion.32
  10.9 0.0 all-reduce.4.cloned.1.call-update
  10.9 0.0 all-reduce.6.cloned.1.call-start
  11.0 3.4 reduce-window.6
  14.4 0.1 slice.54
  14.4 0.1 copy.4
  14.6 0.1 copy.5
  14.7 0.1 broadcast_add_fusion
  14.8 276.1 %all-reduce.4.cloned.1.call-done = f32[256,1024]{1,0:T(8,128)} async-done(((f32[256,1024]{1,0:T(8,128)}), f32[256,1024]{1,0:T(8,128)}) %all-reduce.4.cloned.1.call-update) | async-done | bytes 1048592 | tf_op jit(solution)/shard_map/psum | solution.py:12
  290.9 2.6 fusion.33
  293.5 0.8 copy.6
  294.4 1.0 fusion.9
  295.4 0.0 copy-start.6
  295.4 0.7 copy-done.6
  296.1 11.7 %cholesky.130 = f32[128,128]{1,0:T(8,128)S(1)} custom-call(f32[128,128]{1,0:T(8,128)S(1)} %cholesky.194), custom_call_target="Cholesky" | custom-call | tf_op jit(solution)/shard_map/jit(cholesky)/cholesky | solution.py:16
  307.8 10.4 %custom-call.13 = f32[1,128,128]{1,2,0:T(8,128)} custom-call(f32[1,128,128]{2,1,0:T(8,128)S(1)} %get-tuple-element.50), custom_call_target="InvertDiagBlocksLowerTriangular" | custom-call | tf_op jit(solution)/shard_map/jit(cholesky)/cholesky | solution.py:16
  318.3 1.1 constant_dynamic-update-slice_fusion.3
  319.4 1.7 convolution_subtract_fusion.3
  321.1 12.5 %cholesky.147 = f32[128,128]{1,0:T(8,128)S(1)} custom-call(f32[128,128]{1,0:T(8,128)} %convolution_subtract_fusion.3), custom_call_target="Cholesky" | custom-call | tf_op jit(solution)/shard_map/jit(cholesky)/cholesky | solution.py:16
  333.7 0.7 compare_reduce_fusion.2
  335.7 1.0 select_select_fusion.1
  336.7 0.1 triangular_solve.75
  336.8 0.7 broadcast.147.clone
  337.4 5.4 while.4
  337.4 0.7 fusion.54
  338.1 2.0 bitcast_dynamic-update-slice_fusion.4
  340.1 0.7 fusion.54
  340.8 2.0 bitcast_dynamic-update-slice_fusion.4
  342.8 21.4 %custom-call.14 = f32[2,128,128]{1,2,0:T(8,128)} custom-call(f32[2,128,128]{2,1,0:T(8,128)} %get-tuple-element.21), custom_call_target="InvertDiagBlocksLowerTriangular" | custom-call | tf_op jit(solution)/shard_map/jit(_solve_triangular)/triangular_solve | solution.py:17
  364.2 1.5 fusion.4
  365.8 0.6 convolution_subtract_fusion.1
  366.4 0.2 copy-done.3
  366.6 0.6 fusion.15
  367.2 3.3 fusion.1
  370.5 0.0 all-reduce.6.cloned.1.call-update
  370.6 268.8 %all-reduce.6.cloned.1.call-done = f32[256,1024]{1,0:T(8,128)} async-done(((f32[256,1024]{1,0:T(8,128)}), f32[256,1024]{1,0:T(8,128)}) %all-reduce.6.cloned.1.call-update) | async-done | bytes 1048592 | tf_op jit(solution)/shard_map/psum | solution.py:12
  639.4 2.6 fusion.34
  642.0 0.8 copy.7
  642.9 1.0 fusion.8
  643.9 0.0 copy-start.7
  643.9 0.7 copy-done.7
  644.6 11.7 %cholesky.164 = f32[128,128]{1,0:T(8,128)S(1)} custom-call(f32[128,128]{1,0:T(8,128)S(1)} %cholesky.197), custom_call_target="Cholesky" | custom-call | tf_op jit(solution)/shard_map/jit(cholesky)/cholesky | solution.py:16
  656.3 9.8 %custom-call.15 = f32[1,128,128]{1,2,0:T(8,128)S(1)} custom-call(f32[1,128,128]{2,1,0:T(8,128)S(1)} %get-tuple-element.46), custom_call_target="InvertDiagBlocksLowerTriangular" | custom-call | tf_op jit(solution)/shard_map/jit(cholesky)/cholesky | solution.py:16
  666.2 1.0 constant_dynamic-update-slice_fusion.1
  667.2 1.1 convolution_subtract_fusion.2
  668.3 11.9 %cholesky.181 = f32[128,128]{1,0:T(8,128)S(1)} custom-call(f32[128,128]{1,0:T(8,128)S(1)} %convolution_subtract_fusion.2), custom_call_target="Cholesky" | custom-call | tf_op jit(solution)/shard_map/jit(cholesky)/cholesky | solution.py:16
  680.2 0.6 compare_reduce_fusion
  680.9 0.7 compare_reduce_fusion.1
  682.8 1.0 select_select_fusion
  683.9 4.1 while.5
  683.9 0.6 fusion.55
  684.5 1.4 bitcast_dynamic-update-slice_fusion.5
  685.9 0.6 fusion.55
  686.5 1.4 bitcast_dynamic-update-slice_fusion.5
  688.0 20.3 %custom-call.16 = f32[2,128,128]{1,2,0:T(8,128)} custom-call(f32[2,128,128]{2,1,0:T(8,128)S(1)} %get-tuple-element.22), custom_call_target="InvertDiagBlocksLowerTriangular" | custom-call | tf_op jit(solution)/shard_map/jit(_solve_triangular)/triangular_solve | solution.py:17
  708.3 1.5 fusion.2
  709.8 0.6 convolution_subtract_fusion
  710.4 0.6 fusion.11
  711.0 0.8 fusion
  711.8 1.0 copy.8
  712.8 5.7 scatter_custom_fusion
  718.5 34.4 %all_to_all.12 = bf16[16,128,256]{2,1,0:T(8,128)(2,1)S(1)} all-to-all(bf16[16,128,256]{2,1,0:T(8,128)(2,1)S(1)} %bitcast.87), channel_id=1, replica_groups=mesh['sk'=32,'lang'=16] {'lang'}, dimensions={0} | all-to-all | bytes 2097152 | tf_op jit(solution)/shard_map/all_to_all | solution.py:44
  752.9 1.0 copy.34
  (39 shorter events, 0.4 us)
Async XLA Ops:
  6.5 1.6 copy-start
  6.5 4.4 copy-start.10
  6.5 284.4 %all-reduce.4.cloned.1.call-start = ((), (), s32[]{:S(2)}) async-start(), calls=%async_computation.1 | async-start | bytes 2097152 | tf_op jit(solution)/shard_map/psum | solution.py:12
  10.9 628.6 %all-reduce.6.cloned.1.call-start = ((), (), s32[]{:S(2)}) async-start(), calls=%async_computation.2 | async-start | bytes 2097152 | tf_op jit(solution)/shard_map/psum | solution.py:12
  293.5 70.7 %copy-start.1 = (f32[256,1024]{1,0:T(8,128)S(1)}, f32[256,1024]{1,0:T(8,128)}, u32[]{:S(2)}) copy-start(f32[256,1024]{1,0:T(8,128)} %all-reduce.4.cloned.1.call-done) | copy-start | bytes 3145732
  295.4 0.7 copy-start.6
  333.7 2.0 copy-start.5
  364.2 2.3 copy-start.8
  365.8 0.8 copy-start.3
  642.0 66.2 %copy-start.2 = (f32[256,1024]{1,0:T(8,128)S(1)}, f32[256,1024]{1,0:T(8,128)}, u32[]{:S(2)}) copy-start(f32[256,1024]{1,0:T(8,128)} %all-reduce.6.cloned.1.call-done) | copy-start | bytes 3145732
  643.9 0.7 copy-start.7
  680.2 2.6 copy-start.4
  708.3 2.1 copy-start.9
Sparse Core Ops, SparseCore 0:
  12.4 278.4 all-reduce.3
  370.6 268.7 all-reduce.5
where the time goes:
time: 775 us; the launch traced here: 761 us
  waiting for transfers between devices  545 us (70%)
  other arithmetic  120 us (15%)
  blocking collectives  34.4 us (4%)
  local copies, waits for them, and re-layouts  23.1 us (3%)
  matrix products  22.4 us (3%)
  between operations  16.4 us (2%)
    psum x2, waiting for transfers between devices, orthonormal(): sketch = lax.psum(term, ('sk', 'lang'))  545 us
    another operation x13, other arithmetic, orthonormal(): lower_factor = jnp.linalg.cholesky(gram_matrix)  70.3 us
    another operation x5, other arithmetic, orthonormal(): jax.scipy.linalg.solve_triangular(lower_factor, sketch, lower=True)  43.7 us
    all_to_all x1, blocking collectives, on_device(): lax.all_to_all(outgoing, 'lang', split_axis=0, concat_axis=0, tiled=True)  34.4 us
  transfers between devices with their start and end apart: 2, of which 2 were waited for; matrix products, arithmetic and copies ran while one was open for 1% of the time, Pallas kernels for 0%

commit v1 on v0

--- a/solution.py
+++ b/solution.py
@@ -8,8 +8,17 @@
 CAP = 128
 
 
+def all_sum(term):
+    axes = ("sk", "lang")
+    count = lax.axis_size("sk") * lax.axis_size("lang")
+    pieces = term.reshape(count, -1)
+    slice_sum = jnp.sum(lax.all_to_all(pieces, axes, 0, 0, tiled=True), axis=0, keepdims=True)
+    spread = jnp.broadcast_to(slice_sum, pieces.shape)
+    return lax.all_to_all(spread, axes, 0, 0, tiled=True).reshape(term.shape)
+
+
 def orthonormal(term):
-    sketch = lax.psum(term, ("sk", "lang"))
+    sketch = all_sum(term)
     gram_matrix = jnp.dot(
         sketch, sketch.T, precision=lax.Precision.HIGHEST, preferred_element_type=jnp.float32
     )

time: 775 us -> 397 us (0.51)
  waiting for transfers between devices: 545 us -> 92.7 us
  blocking collectives: 34.4 us -> 76.1 us
  starting transfers between devices: 0.04 us -> 41.3 us
  between operations: 16.4 us -> 3.03 us
  local copies, waits for them, and re-layouts: 23.1 us -> 31.6 us
    psum x2 -> x0, waiting for transfers between devices: 545 us -> none  [orthonormal(): sketch = lax.psum(term, ('sk', 'lang'))]
    all_to_all x0 -> x3, waiting for transfers between devices: none -> 92.7 us  [the longest x2 60.4 us: all_sum(): return lax.all_to_all(spread, axes, 0, 0, tiled=True).reshape(term.shape)]
    all_to_all x0 -> x1, blocking collectives: none -> 42.1 us  [all_sum(): lax.all_to_all(pieces, axes, 0, 0, tiled=True)]
    all_to_all x0 -> x3, starting transfers between devices: none -> 41.3 us  [the longest x1 22.2 us: all_sum(): lax.all_to_all(pieces, axes, 0, 0, tiled=True)]
  transfers between devices with their start and end apart: 2 -> 3, of which waited for: 2 -> 3; matrix products, arithmetic and copies ran while one was open for 1% -> 1% of each run, Pallas kernels for 0% -> 0%
where the time goes in v1:
time: 397 us; the launch traced here: 390 us
  other arithmetic  127 us (32%)
  waiting for transfers between devices  92.7 us (23%)
  blocking collectives  76.1 us (19%)
  starting transfers between devices  41.3 us (10%)
  local copies, waits for them, and re-layouts  31.6 us (8%)
  matrix products  17.7 us (4%)
    another operation x13, other arithmetic, orthonormal(): lower_factor = jnp.linalg.cholesky(gram_matrix)  69.2 us
    all_to_all x2, waiting for transfers between devices, all_sum(): return lax.all_to_all(spread, axes, 0, 0, tiled=True).reshape(term.shape)  60.4 us
    another operation x5, other arithmetic, orthonormal(): jax.scipy.linalg.solve_triangular(lower_factor, sketch, lower=True)  42.6 us
    all_to_all x1, blocking collectives, all_sum(): lax.all_to_all(pieces, axes, 0, 0, tiled=True)  42.1 us
    all_to_all x1, blocking collectives, on_device(): lax.all_to_all(outgoing, 'lang', split_axis=0, concat_axis=0, tiled=True)  34 us
    all_to_all x1, waiting for transfers between devices, all_sum(): lax.all_to_all(pieces, axes, 0, 0, tiled=True)  32.3 us
    all_to_all x1, starting transfers between devices, all_sum(): lax.all_to_all(pieces, axes, 0, 0, tiled=True)  22.2 us
    all_to_all x2, starting transfers between devices, all_sum(): return lax.all_to_all(spread, axes, 0, 0, tiled=True).reshape(term.shape)  19.1 us
  transfers between devices with their start and end apart: 3, of which 3 were waited for; matrix products, arithmetic and copies ran while one was open for 1% of the time, Pallas kernels for 0%

profile of v1, /device:TPU:1, one launch (start us, length us, event | category | flops | bytes accessed | tf_op | source)
XLA Modules:
  0.0 389.8 jit_solution(2129844659503639780)
XLA Ops:
  0.0 1.6 copy-done
  1.6 1.8 fusion.32
  3.4 2.2 all_to_all.37
  5.6 22.2 %all-to-all-start = ((f32[512,1,512]{2,1,0:T(1,128)}), f32[512,1,512]{2,1,0:T(1,128)S(1)}, u32[]{:S(2)}, u32[]{:S(2)}) async-start(f32[512,1,512]{2,1,0:T(1,128)} %all_to_all.37), calls=%async_computation | async-start | bytes 2097152 | tf_op jit(solution)/shard_map/all_to_all | solution.py:15
  27.7 32.3 %all-to-all-done = f32[512,1,512]{2,1,0:T(1,128)S(1)} async-done(((f32[512,1,512]{2,1,0:T(1,128)}), f32[512,1,512]{2,1,0:T(1,128)S(1)}, u32[]{:S(2)}, u32[]{:S(2)}) %all-to-all-start) | async-done | bytes 1048608 | tf_op jit(solution)/shard_map/all_to_all | solution.py:15
  60.1 0.6 reduce_sum.28
  60.7 1.5 broadcast_in_dim.8
  62.2 9.7 %all-to-all-start.1 = ((f32[512,1,512]{2,1,0:T(1,128)}), f32[512,1,512]{2,1,0:T(1,128)S(1)}, u32[]{:S(2)}, u32[]{:S(2)}) async-start(f32[512,1,512]{2,1,0:T(1,128)} %broadcast_in_dim.8), calls=%async_computation.1 | async-start | bytes 2097152 | tf_op jit(solution)/shard_map/all_to_all | solution.py:17
  71.9 32.1 %all-to-all-done.1 = f32[512,1,512]{2,1,0:T(1,128)S(1)} async-done(((f32[512,1,512]{2,1,0:T(1,128)}), f32[512,1,512]{2,1,0:T(1,128)S(1)}, u32[]{:S(2)}, u32[]{:S(2)}) %all-to-all-start.1) | async-done | bytes 1048608 | tf_op jit(solution)/shard_map/all_to_all | solution.py:17
  104.0 3.7 reduce.10
  107.7 1.6 reshape.71
  109.3 1.0 fusion.33
  110.3 0.8 copy.12
  111.2 1.0 fusion.9
  112.2 0.7 copy-done.4
  112.9 11.7 %cholesky.130 = f32[128,128]{1,0:T(8,128)S(1)} custom-call(f32[128,128]{1,0:T(8,128)S(1)} %cholesky.194), custom_call_target="Cholesky" | custom-call | tf_op jit(solution)/shard_map/jit(cholesky)/cholesky | solution.py:25
  124.6 9.8 %custom-call.13 = f32[1,128,128]{1,2,0:T(8,128)S(1)} custom-call(f32[1,128,128]{2,1,0:T(8,128)S(1)} %get-tuple-element.50), custom_call_target="InvertDiagBlocksLowerTriangular" | custom-call | tf_op jit(solution)/shard_map/jit(cholesky)/cholesky | solution.py:25
  134.4 1.0 constant_dynamic-update-slice_fusion.3
  135.5 1.1 convolution_subtract_fusion.3
  136.6 12.1 %cholesky.147 = f32[128,128]{1,0:T(8,128)S(1)} custom-call(f32[128,128]{1,0:T(8,128)S(1)} %convolution_subtract_fusion.3), custom_call_target="Cholesky" | custom-call | tf_op jit(solution)/shard_map/jit(cholesky)/cholesky | solution.py:25
  148.8 0.7 compare_reduce_fusion.2
  150.6 1.0 select_select_fusion.1
  151.7 3.8 while.4
  151.7 0.6 fusion.54
  152.3 1.3 bitcast_dynamic-update-slice_fusion.4
  154.2 1.3 bitcast_dynamic-update-slice_fusion.4
  155.5 20.3 %custom-call.14 = f32[2,128,128]{1,2,0:T(8,128)} custom-call(f32[2,128,128]{2,1,0:T(8,128)S(1)} %get-tuple-element.21), custom_call_target="InvertDiagBlocksLowerTriangular" | custom-call | tf_op jit(solution)/shard_map/jit(_solve_triangular)/triangular_solve | solution.py:26
  175.8 1.5 fusion.4
  178.2 0.6 fusion.15
  178.8 3.3 fusion.1
  182.1 2.5 all_to_all.38
  184.6 42.1 %all_to_all.45 = f32[512,1,512]{2,1,0:T(1,128)} all-to-all(f32[512,1,512]{2,1,0:T(1,128)S(1)} %all_to_all.38), channel_id=1, replica_groups=mesh['sk'=32,'lang'=16] {'sk','lang'}, dimensions={0} | all-to-all | bytes 2097152 | tf_op jit(solution)/shard_map/all_to_all | solution.py:15
  226.7 1.9 reduce_sum.29
  228.5 1.5 broadcast_in_dim.9
  230.0 9.5 %all-to-all-start.3 = ((f32[512,1,512]{2,1,0:T(1,128)}), f32[512,1,512]{2,1,0:T(1,128)S(1)}, u32[]{:S(2)}, u32[]{:S(2)}) async-start(f32[512,1,512]{2,1,0:T(1,128)} %broadcast_in_dim.9), calls=%async_computation.3 | async-start | bytes 2097152 | tf_op jit(solution)/shard_map/all_to_all | solution.py:17
  239.5 3.5 reduce-window.6
  243.6 28.2 %all-to-all-done.3 = f32[512,1,512]{2,1,0:T(1,128)S(1)} async-done(((f32[512,1,512]{2,1,0:T(1,128)}), f32[512,1,512]{2,1,0:T(1,128)S(1)}, u32[]{:S(2)}, u32[]{:S(2)}) %all-to-all-start.3) | async-done | bytes 1048608 | tf_op jit(solution)/shard_map/all_to_all | solution.py:17
  271.8 3.7 reduce.11
  275.5 1.6 reshape.72
  277.1 1.0 fusion.34
  278.1 0.8 copy.14
  279.0 1.0 fusion.8
  280.0 0.7 copy-done.5
  280.7 11.7 %cholesky.164 = f32[128,128]{1,0:T(8,128)S(1)} custom-call(f32[128,128]{1,0:T(8,128)S(1)} %cholesky.197), custom_call_target="Cholesky" | custom-call | tf_op jit(solution)/shard_map/jit(cholesky)/cholesky | solution.py:25
  292.4 9.8 %custom-call.15 = f32[1,128,128]{1,2,0:T(8,128)S(1)} custom-call(f32[1,128,128]{2,1,0:T(8,128)S(1)} %get-tuple-element.46), custom_call_target="InvertDiagBlocksLowerTriangular" | custom-call | tf_op jit(solution)/shard_map/jit(cholesky)/cholesky | solution.py:25
  302.3 1.0 constant_dynamic-update-slice_fusion.1
  303.3 1.1 convolution_subtract_fusion.2
  304.4 11.9 %cholesky.181 = f32[128,128]{1,0:T(8,128)S(1)} custom-call(f32[128,128]{1,0:T(8,128)S(1)} %convolution_subtract_fusion.2), custom_call_target="Cholesky" | custom-call | tf_op jit(solution)/shard_map/jit(cholesky)/cholesky | solution.py:25
  316.4 0.6 compare_reduce_fusion
  317.0 0.7 compare_reduce_fusion.1
  319.0 1.0 select_select_fusion
  320.0 4.1 %while.5 = (s32[]{:T(128)}, f32[256,256]{1,0:T(8,128)S(1)}, s32[2,2]{1,0:T(2,128)S(1)}, f32[2,128,128]{2,1,0:T(8,128)S(1)}, s32[]{:T(128)}) while((s32[]{:T(128)}, f32[256,256]{1,0:T(8,128)S(1)}, s32[2,2]{1,0:T(2,128)S(1)}, f32[2,128,128]{2,1,0:T(8,128)S(1)}, s32[]{:T(128)}) %tuple.49), condition=%wide.while_cond.clone, body=%wide.while_body.clone.sunk | while | flops 2 | bytes 131181 | solution.py:26
  320.0 0.6 fusion.55
  320.6 1.4 bitcast_dynamic-update-slice_fusion.5
  322.1 0.6 fusion.55
  322.7 1.4 bitcast_dynamic-update-slice_fusion.5
  324.1 20.3 %custom-call.16 = f32[2,128,128]{1,2,0:T(8,128)} custom-call(f32[2,128,128]{2,1,0:T(8,128)S(1)} %get-tuple-element.22), custom_call_target="InvertDiagBlocksLowerTriangular" | custom-call | tf_op jit(solution)/shard_map/jit(_solve_triangular)/triangular_solve | solution.py:26
  344.4 1.5 fusion.2
  346.5 0.6 fusion.11
  347.2 0.8 fusion
  347.9 1.0 copy.15
  348.9 5.7 %scatter_custom_fusion = bf16[2048,256]{1,0:T(8,128)(2,1)S(1)} fusion(s32[1024]{0:T(1024)S(1)} %bitcast.95, bf16[1024,256]{1,0:T(8,128)(2,1)} %copy.15, bf16[]{:T(256)} %constant.92.clone.1), kind=kCustom, calls=%fused_computation.19 | custom fusion | bytes 1049088 | tf_op jit(solution)/shard_map/scatter | solution.py:51
  354.6 34.0 %all_to_all.44 = bf16[16,128,256]{2,1,0:T(8,128)(2,1)S(1)} all-to-all(bf16[16,128,256]{2,1,0:T(8,128)(2,1)S(1)} %bitcast.87), channel_id=1, replica_groups=mesh['sk'=32,'lang'=16] {'lang'}, dimensions={0} | all-to-all | bytes 2097152 | tf_op jit(solution)/shard_map/all_to_all | solution.py:53
  388.6 1.0 copy.41
  (46 shorter events, 2.8 us)
Async XLA Ops:
  0.0 1.6 copy-start
  5.6 54.5 %all-to-all-start = ((f32[512,1,512]{2,1,0:T(1,128)}), f32[512,1,512]{2,1,0:T(1,128)S(1)}, u32[]{:S(2)}, u32[]{:S(2)}) async-start(f32[512,1,512]{2,1,0:T(1,128)} %all_to_all.37), calls=%async_computation | async-start | bytes 2097152 | tf_op jit(solution)/shard_map/all_to_all | solution.py:15
  62.2 41.8 %all-to-all-start.1 = ((f32[512,1,512]{2,1,0:T(1,128)}), f32[512,1,512]{2,1,0:T(1,128)S(1)}, u32[]{:S(2)}, u32[]{:S(2)}) async-start(f32[512,1,512]{2,1,0:T(1,128)} %broadcast_in_dim.8), calls=%async_computation.1 | async-start | bytes 2097152 | tf_op jit(solution)/shard_map/all_to_all | solution.py:17
  112.1 0.7 copy-start.4
  148.7 1.9 copy-start.3
  175.8 2.3 copy-start.6
  177.4 0.8 copy-start.1
  226.7 12.9 %copy-start.8 = (s32[1024,1]{0,1:T(1,128)S(1)}, s32[1024,1]{0,1:T(1,128)}, u32[]{:S(2)}) copy-start(s32[1024,1]{0,1:T(1,128)} %param.8) | copy-start | bytes 12292
  230.0 41.8 %all-to-all-start.3 = ((f32[512,1,512]{2,1,0:T(1,128)}), f32[512,1,512]{2,1,0:T(1,128)S(1)}, u32[]{:S(2)}, u32[]{:S(2)}) async-start(f32[512,1,512]{2,1,0:T(1,128)} %broadcast_in_dim.9), calls=%async_computation.3 | async-start | bytes 2097152 | tf_op jit(solution)/shard_map/all_to_all | solution.py:17
  280.0 0.7 copy-start.5
  316.4 2.6 copy-start.2
  344.4 2.1 copy-start.7
